TPU v7x, 512 devices: a whole 4x8x8 slice. The times are simulated.
512 devices in a mesh: row: 32 (over z_hi, y), col: 16 (over x, z_lo, core).
Axes of the slice: x: 4, y: 8, z: 8 (z_hi: 4, z_lo: 2; z = z_hi * 2 + z_lo), core: 2. Of those that a mesh axis runs over, the one named last changes fastest.
Arguments:
- s_rows: bfloat16 [32768, 1024], P('row', 'col'), may hold values from -0.1875 to 0.1875
- iterate: bfloat16 [1024, 32768], P('row', 'col'), may hold values from -6 to 6
Outputs:
- product: bfloat16 [32768, 32768], P('row', 'col')
All inputs are finite; a program needn't handle non-finite values.
Results may differ from a plain program's by a relative error of at most 0.001.
Values may be sent and summed in bfloat16 or wider, within the bound.
No kernel may reach another device: no remote copies, remote signals or barrier semaphores. Data moves between devices by JAX's collectives and lax.ppermute only.
A program may use at most 64 MiB of HBM per device.

v0:
```python
import jax
import jax.numpy as jnp
from jax import lax
from jax.sharding import Mesh, PartitionSpec as P

ROW = ("z_hi", "y")
COL = ("x", "z_lo", "core")


def shards(s_rows, iterate):
    panel = lax.all_gather(s_rows, COL, axis=1, tiled=True)
    nz, ny = (lax.axis_size("z_hi"), lax.axis_size("y"))
    w = lax.all_gather(iterate, "z_hi", axis=0, tiled=False)
    w = lax.all_gather(w, "y", axis=0, tiled=False)
    s4 = panel.reshape(panel.shape[0], nz, ny, -1)
    product = jnp.einsum("rzyk,yzkc->rc", s4, w, preferred_element_type=jnp.float32)
    return product.astype(jnp.bfloat16)


def solution(mesh):
    nr, nc = mesh.devices.shape
    devs = mesh.devices.reshape(4, nr // 4, nc // 4, 2, 2)
    m = Mesh(devs, ROW + COL)
    return jax.shard_map(
        shards, mesh=m, in_specs=(P(ROW, COL), P(ROW, COL)), out_specs=P(ROW, COL), check_vma=False
    )
```

profile of v0, /device:TPU:1, one launch (start us, length us, event | category | flops | bytes accessed | tf_op | source)
XLA Modules:
  0.0 129.2 jit_solution(9073005861399664550)
XLA Ops:
  6.5 0.0 all-gather.5.cloned.1.call-start
  6.5 0.7 all-gather.5.cloned.1.call-update
  7.3 0.0 all-gather.7.cloned.1.call-start
  7.3 21.6 %all-gather = bf16[128,2048]{1,0:T(8,128)(2,1)} all-gather(bf16[32,2048]{1,0:T(8,128)(2,1)} %param.3), channel_id=2, replica_groups=mesh['z_hi'=4,'y'=8,'x'=4,'z_lo'=2,'core'=2] {'z_hi'}, dimensions={0}, use_global_device_ids=true | all-gather | bytes 655360 | tf_op jit(solution)/shard_map/all_gather | solution.py:13
  28.9 0.0 all-gather.7.cloned.1.call-update
  28.9 25.8 %all-gather.5.cloned.1.call-done = bf16[1024,1024]{0,1:T(8,128)(2,1)} async-done(((bf16[1024,64]{0,1:T(8,128)(2,1)}), bf16[1024,1024]{0,1:T(8,128)(2,1)}) %all-gather.5.cloned.1.call-update) | async-done | bytes 2097168 | tf_op jit(solution)/shard_map/all_gather | solution.py:11
  54.7 58.3 %all-gather.7.cloned.1.call-done = bf16[32,32,2048]{2,1,0:T(8,128)(2,1)} async-done(((bf16[4,32,2048]{2,1,0:T(8,128)(2,1)}), bf16[32,32,2048]{2,1,0:T(8,128)(2,1)}) %all-gather.7.cloned.1.call-update) | async-done | bytes 4194320 | tf_op jit(solution)/shard_map/all_gather | solution.py:14
  113.0 9.4 %bitcast_convert_fusion = bf16[1024,2048]{1,0:T(8,128)(2,1)} fusion(bf16[8,4,32,2048]{3,2,1,0:T(8,128)(2,1)} %bitcast.9, bf16[1024,4,8,32]{0,3,2,1:T(8,128)(2,1)} %bitcast.10), kind=kOutput, calls=%fused_computation | convolution fusion | flops 4297064448 | bytes 10485760 | tf_op jit(solution)/shard_map/rzyk,yzkc->rc/dot_general | solution.py:16
Async XLA Ops:
  6.5 48.2 %all-gather.5.cloned.1.call-start = ((), (), s32[]{:S(2)}) async-start(), calls=%async_computation | async-start | bytes 2228224 | tf_op jit(solution)/shard_map/all_gather | solution.py:11
  7.3 105.7 %all-gather.7.cloned.1.call-start = ((), (), s32[]{:S(2)}) async-start(), calls=%async_computation.1 | async-start | bytes 4718592 | tf_op jit(solution)/shard_map/all_gather | solution.py:14
Sparse Core Ops, SparseCore 0:
  9.5 45.1 all-gather.4
  56.8 56.1 all-gather.6
where the time goes:
time: 129 us
  waiting for transfers between devices  84.8 us (66%)
  blocking collectives  21.6 us (17%)
  between operations  13.4 us (10%)
  matrix products  9.41 us (7%)
    all_gather x1, waiting for transfers between devices, shards(): w = lax.all_gather(w, 'y', axis=0, tiled=False)  58.3 us
    all_gather x1, waiting for transfers between devices, shards(): panel = lax.all_gather(s_rows, COL, axis=1, tiled=True)  25.8 us
    all_gather x1, blocking collectives, shards(): w = lax.all_gather(iterate, 'z_hi', axis=0, tiled=False)  21.6 us
    dot_general x1, matrix products, shards(): jnp.einsum('rzyk,yzkc->rc', s4, w, preferred_element_type=jnp.float32)  9.41 us
  transfers between devices with their start and end apart: 2, of which 2 were waited for; matrix products, arithmetic and copies ran while one was open for 0% of the time, Pallas kernels for 0%

commit v1 on v0

--- a/solution.py
+++ b/solution.py
@@ -8,7 +8,9 @@
 
 
 def shards(s_rows, iterate):
-    panel = lax.all_gather(s_rows, COL, axis=1, tiled=True)
+    panel = jnp.concatenate(
+        lax.all_to_all(jnp.stack([s_rows] * lax.axis_size(COL)), COL, 0, 0), axis=1
+    )
     nz, ny = (lax.axis_size("z_hi"), lax.axis_size("y"))
     w = lax.all_gather(iterate, "z_hi", axis=0, tiled=False)
     w = lax.all_gather(w, "y", axis=0, tiled=False)

time: 129 us -> 102 us (0.79)
  waiting for transfers between devices: 84.8 us -> 22.2 us
  blocking collectives: 21.6 us -> 57.2 us
    all_gather x1, waiting for transfers between devices: 58.3 us -> 22.2 us  [shards(): w = lax.all_gather(w, 'y', axis=0, tiled=False)]
    all_to_all x0 -> x1, blocking collectives: none -> 35.7 us  [shards(): lax.all_to_all(jnp.stack([s_rows] * lax.axis_size(COL)), COL, 0, 0)]
    all_gather x1 -> x0, waiting for transfers between devices: 25.8 us -> none  [shards(): panel = lax.all_gather(s_rows, COL, axis=1, tiled=True)]
  transfers between devices with their start and end apart: 2 -> 1, of which waited for: 2 -> 1; matrix products, arithmetic and copies ran while one was open for 0% -> 1% of each run, Pallas kernels for 0% -> 0%
where the time goes in v1:
time: 102 us
  blocking collectives  57.2 us (56%)
  waiting for transfers between devices  22.2 us (22%)
  between operations  13.4 us (13%)
  matrix products  8.31 us (8%)
  local copies, waits for them, and re-layouts  1.16 us (1%)
    all_to_all x1, blocking collectives, shards(): lax.all_to_all(jnp.stack([s_rows] * lax.axis_size(COL)), COL, 0, 0)  35.7 us
    all_gather x1, waiting for transfers between devices, shards(): w = lax.all_gather(w, 'y', axis=0, tiled=False)  22.2 us
    all_gather x1, blocking collectives, shards(): w = lax.all_gather(iterate, 'z_hi', axis=0, tiled=False)  21.6 us
    dot_general x1, matrix products, shards(): jnp.einsum('rzyk,yzkc->rc', s4, w, preferred_element_type=jnp.float32)  8.31 us
  transfers between devices with their start and end apart: 1, of which 1 were waited for; matrix products, arithmetic and copies ran while one was open for 1% of the time, Pallas kernels for 0%

profile of v1, /device:TPU:1, one launch (start us, length us, event | category | flops | bytes accessed | tf_op | source)
XLA Modules:
  0.0 102.3 jit_solution(6217019091884960823)
XLA Ops:
  6.5 0.0 all-gather.4.cloned.1.call-start
  6.5 21.6 %all-gather = bf16[128,2048]{1,0:T(8,128)(2,1)} all-gather(bf16[32,2048]{1,0:T(8,128)(2,1)} %param.3), channel_id=2, replica_groups=mesh['z_hi'=4,'y'=8,'x'=4,'z_lo'=2,'core'=2] {'z_hi'}, dimensions={0}, use_global_device_ids=true | all-gather | bytes 655360 | tf_op jit(solution)/shard_map/all_gather | solution.py:15
  28.1 0.0 all-gather.4.cloned.1.call-update
  28.1 1.2 %stack.2 = bf16[16,1024,64]{1,2,0:T(8,128)(2,1)S(1)} broadcast(bf16[1024,64]{0,1:T(8,128)(2,1)} %param.2), dimensions={1,2} | broadcast | bytes 2228224 | tf_op jit(solution)/shard_map/stack | solution.py:12
  29.3 35.7 %all_to_all.5 = bf16[16,1024,64]{1,2,0:T(8,128)(2,1)S(1)} all-to-all(bf16[16,1024,64]{1,2,0:T(8,128)(2,1)S(1)} %stack.2), channel_id=1, replica_groups=mesh['z_hi'=4,'y'=8,'x'=4,'z_lo'=2,'core'=2] {'x','z_lo','core'}, dimensions={0} | all-to-all | bytes 4194304 | tf_op jit(solution)/shard_map/all_to_all | solution.py:12
  64.9 22.2 %all-gather.4.cloned.1.call-done = bf16[32,32,2048]{2,1,0:T(8,128)(2,1)} async-done(((bf16[4,32,2048]{2,1,0:T(8,128)(2,1)}), bf16[32,32,2048]{2,1,0:T(8,128)(2,1)}) %all-gather.4.cloned.1.call-update) | async-done | bytes 4194320 | tf_op jit(solution)/shard_map/all_gather | solution.py:16
  87.1 8.3 %bitcast_convert_fusion = bf16[1024,2048]{1,0:T(8,128)(2,1)} fusion(bf16[8,4,32,2048]{3,2,1,0:T(8,128)(2,1)} %bitcast.12, bf16[1024,4,8,32]{0,3,2,1:T(8,128)(2,1)S(1)} %bitcast.11), kind=kOutput, calls=%fused_computation | convolution fusion | flops 4297064448 | bytes 10485760 | tf_op jit(solution)/shard_map/rzyk,yzkc->rc/dot_general | solution.py:18
Async XLA Ops:
  6.5 80.6 %all-gather.4.cloned.1.call-start = ((), (), s32[]{:S(2)}) async-start(), calls=%async_computation.1 | async-start | bytes 4718592 | tf_op jit(solution)/shard_map/all_gather | solution.py:16
Sparse Core Ops, SparseCore 0:
  28.2 58.8 all-gather.3
